TPU v7x, 32 devices: a whole 2x2x4 slice. The times are simulated.
32 devices in a mesh: group: 2 (over y), seq: 8 (over z, x), chan: 2 (over core).
Axes of the slice: x: 2, y: 2, z: 4, core: 2. Of those that a mesh axis runs over, the one named last changes fastest.
Arguments:
- fresh: bfloat16 [2048, 3, 2048], P(('group', 'seq'), None, 'chan'), parts along dimension 0, may hold values from -6 to 6
- library: bfloat16 [8, 8, 2048], P('seq', None, 'chan'), may hold values from -6 to 6
- block_slot: int32 [8], replicated, may hold values from 0 to 7, each once
- prefix_blocks: int32 [16, 4], P('group'), parts along dimension 0, may hold values from 0 to 7, all different within a row
- short_taps: float32 [3, 3, 2048], P(None, None, 'chan'), may hold values from -4 to 4
- long_filter: float32 [1024, 2048], P('seq', 'chan'), may hold values from -2 to 2
- skip_gain: float32 [2048], P('chan'), may hold values from -6 to 6
Outputs:
- mixed: bfloat16 [2048, 2048], P(('group', 'seq'), 'chan'), parts along dimension 0
There are 2 independent parts, one for each index of `group`. A program takes and returns all parts, laid end to end along the dimension named above; an argument that names none is the same for every part. Nothing has to cross between parts.
Inputs may be any that keep to these rules, and one draw needn't show every extreme that they name: `block_slot`: each number appears once. `prefix_blocks`: every library block is named at least once; the four entries of a row differ.
All inputs are finite; a program needn't handle non-finite values.
Results may differ from a plain program's by a relative error of at most 0.008.
Values may be sent and summed in bfloat16 or wider, within the bound.
No kernel may reach another device: no remote copies, remote signals or barrier semaphores. Data moves between devices by JAX's collectives and lax.ppermute only.
A program may use at most 64 MiB of HBM per device.

v0:
```python
import math
import jax
import jax.numpy as jnp
from jax import lax
from jax.sharding import PartitionSpec as P

TAPS = 3
BLK = 8


def from_behind(shard, axis, by):
    count = lax.axis_size(axis)
    pairs = [(i, i + by) for i in range(count) if 0 <= i + by < count]
    return lax.ppermute(shard, axis, pairs)


def exact_dot(pattern, matrix, tensor):
    return jnp.einsum(pattern, matrix, tensor, precision=lax.Precision.HIGHEST)


def turn_angles(numbers, period):
    return (numbers % period).astype(jnp.float32) * (2.0 * math.pi / period)


def ring_body(fresh, library, block_slot, prefix_blocks, short_taps, long_filter, skip_gain):
    row_count = fresh.shape[0]
    channels = fresh.shape[2]
    devices = lax.axis_size("seq")
    seq_index = lax.axis_index("seq")
    group_rows = row_count // devices
    period = 2 * row_count * devices
    block_ids = jnp.arange(devices, dtype=jnp.int32)
    mode_ids = jnp.arange(2 * devices, dtype=jnp.int32)
    coarse = turn_angles(mode_ids[:, None] * block_ids[None, :], 2 * devices)
    cos_q = jnp.cos(coarse)
    sin_q = jnp.sin(coarse)
    local_rows = seq_index * group_rows + jnp.arange(group_rows, dtype=jnp.int32)
    twist = turn_angles(mode_ids[:, None] * local_rows[None, :], period)
    twist_cos = jnp.cos(twist)[:, :, None]
    twist_sin = jnp.sin(twist)[:, :, None]
    row_ids = jnp.arange(row_count, dtype=jnp.int32)
    fine_angles = turn_angles(row_ids[:, None] * row_ids[None, :], row_count)
    cos_m = jnp.cos(fine_angles)
    sin_m = jnp.sin(fine_angles)
    first_modes = 2 * seq_index + jnp.arange(2, dtype=jnp.int32)
    back_twist = turn_angles(first_modes[:, None] * row_ids[None, :], period)
    back_cos = jnp.cos(back_twist)[:, :, None]
    back_sin = jnp.sin(back_twist)[:, :, None]

    def to_modes(column):
        real_part = exact_dot("kq,qgc->kgc", cos_q, column)
        imag_part = -exact_dot("kq,qgc->kgc", sin_q, column)
        return jnp.stack(
            [
                real_part * twist_cos + imag_part * twist_sin,
                imag_part * twist_cos - real_part * twist_sin,
            ]
        )

    def to_spectrum(spread):
        real_part = exact_dot("ki,jic->jkc", cos_m, spread[0]) + exact_dot(
            "ki,jic->jkc", sin_m, spread[1]
        )
        imag_part = exact_dot("ki,jic->jkc", cos_m, spread[1]) - exact_dot(
            "ki,jic->jkc", sin_m, spread[0]
        )
        return (real_part, imag_part)

    blocks_here = row_count // BLK
    flat_ids = prefix_blocks.reshape(-1)
    first_block = jnp.minimum(seq_index * blocks_here, flat_ids.shape[0] - blocks_here)
    own_ids = lax.dynamic_slice_in_dim(flat_ids, first_block, blocks_here)
    matches = own_ids[:, None] == jnp.arange(block_slot.shape[0], dtype=jnp.int32)[None, :]
    wanted = jnp.sum(jnp.where(matches, block_slot[None, :], 0), axis=1)
    shards = lax.all_gather(library, "seq", axis=0, tiled=True)
    picker = (wanted[:, None] == jnp.arange(shards.shape[0], dtype=jnp.int32)[None, :]).astype(
        jnp.bfloat16
    )
    gathered = jnp.einsum("bn,nlc->blc", picker, shards, preferred_element_type=jnp.float32)
    cached = gathered.reshape(row_count, channels).astype(jnp.bfloat16)
    values = jnp.where(seq_index < devices // 4, cached, fresh[:, 2])
    stacked = jnp.concatenate([fresh[:, :2], values[:, None]], axis=1)
    previous = from_behind(stacked[row_count - (TAPS - 1) :], "seq", 1)
    extended = jnp.concatenate([previous, stacked], axis=0)
    shortened = jnp.zeros((row_count, 3, channels), jnp.float32)
    for offset in range(TAPS):
        window_start = TAPS - 1 - offset
        shortened = shortened + short_taps[offset][None] * extended[
            window_start : window_start + row_count
        ].astype(jnp.float32)
    gating = shortened[:, 0]
    signal = shortened[:, 1] * shortened[:, 2]
    spread_signal = to_modes(
        lax.all_to_all(signal[None], "seq", split_axis=1, concat_axis=0, tiled=True)
    )
    spread_taps = to_modes(
        lax.all_to_all(long_filter[None], "seq", split_axis=1, concat_axis=0, tiled=True)
    )
    moved_signal, moved_taps = (
        lax.all_to_all(
            spread_signal.astype(jnp.bfloat16), "seq", split_axis=1, concat_axis=2, tiled=True
        ).astype(spread_signal.dtype),
        lax.all_to_all(
            spread_taps.astype(jnp.bfloat16), "seq", split_axis=1, concat_axis=2, tiled=True
        ).astype(spread_taps.dtype),
    )
    sig_real, sig_imag = to_spectrum(moved_signal)
    tap_real, tap_imag = to_spectrum(moved_taps)
    prod_real = sig_real * tap_real - sig_imag * tap_imag
    prod_imag = sig_real * tap_imag + sig_imag * tap_real
    back_real = exact_dot("ki,jic->jkc", cos_m, prod_real) - exact_dot(
        "ki,jic->jkc", sin_m, prod_imag
    )
    back_imag = exact_dot("ki,jic->jkc", cos_m, prod_imag) + exact_dot(
        "ki,jic->jkc", sin_m, prod_real
    )
    turned = jnp.stack(
        [back_real * back_cos - back_imag * back_sin, back_imag * back_cos + back_real * back_sin]
    )
    spread = lax.all_to_all(turned, "seq", split_axis=2, concat_axis=1, tiled=True)
    positions = (
        exact_dot("kq,kgc->qgc", cos_q, spread[0]) - exact_dot("kq,kgc->qgc", sin_q, spread[1])
    ) / period
    convolved = lax.all_to_all(positions, "seq", split_axis=0, concat_axis=1, tiled=True)[0]
    output = gating * (convolved + skip_gain[None, :] * signal)
    return output.astype(jnp.bfloat16)


def dft_tables(tokens):
    period = 2 * tokens
    width = 1
    while width * width < tokens:
        width *= 2
    outer = tokens // width
    freqs = jnp.arange(tokens + 1, dtype=jnp.int32)[:, None]
    coarse = turn_angles(freqs * (width * jnp.arange(outer, dtype=jnp.int32))[None, :], period)
    fine = turn_angles(freqs * jnp.arange(width, dtype=jnp.int32)[None, :], period)
    c1, s1 = (jnp.cos(coarse)[:, :, None], jnp.sin(coarse)[:, :, None])
    c2, s2 = (jnp.cos(fine)[:, None, :], jnp.sin(fine)[:, None, :])
    cos_t = (c1 * c2 - s1 * s2).reshape(tokens + 1, tokens)
    sin_t = (s1 * c2 + c1 * s2).reshape(tokens + 1, tokens)
    return (cos_t, sin_t)


def local_body(fresh, library, block_slot, prefix_blocks, short_taps, long_filter, skip_gain):
    row_count, _, channels = fresh.shape
    devices = lax.axis_size("seq")
    seq_index = lax.axis_index("seq")
    tokens = row_count * devices
    own = channels // devices
    lib_here = library.shape[0]
    lib_rows = lib_here * BLK // 4
    packed = jnp.concatenate([fresh, long_filter.astype(jnp.bfloat16)[:, None, :]], axis=1)
    packed = jnp.concatenate([packed, library.reshape(lib_rows, 4, channels)], axis=0)
    moved = lax.all_to_all(packed, "seq", split_axis=2, concat_axis=0, tiled=True)
    moved = moved.reshape(devices, row_count + lib_rows, 4, own)
    rows = moved[:, :row_count].reshape(tokens, 4, own)
    lib_all = moved[:, row_count:].reshape(devices * lib_here, BLK * own)
    slot_ids = block_slot[prefix_blocks.reshape(-1)]
    prefix_len = slot_ids.shape[0] * BLK
    picker = (slot_ids[:, None] == jnp.arange(lib_all.shape[0], dtype=jnp.int32)[None, :]).astype(
        jnp.bfloat16
    )
    cached = jnp.dot(picker, lib_all, preferred_element_type=jnp.float32)
    cached = cached.reshape(prefix_len, own).astype(jnp.bfloat16)
    values = jnp.concatenate([cached, rows[prefix_len:, 2]], axis=0)
    stacked = jnp.concatenate([rows[:, :2], values[:, None]], axis=1).astype(jnp.float32)
    taps = lax.dynamic_slice_in_dim(short_taps, seq_index * own, own, axis=2)
    gain = lax.dynamic_slice_in_dim(skip_gain, seq_index * own, own, axis=0)
    shortened = jnp.zeros((tokens, 3, own), jnp.float32)
    for offset in range(TAPS):
        shifted = jnp.pad(stacked[: tokens - offset], ((offset, 0), (0, 0), (0, 0)))
        shortened = shortened + taps[offset][None] * shifted
    gating = shortened[:, 0]
    signal = shortened[:, 1] * shortened[:, 2]
    cos_t, sin_t = dft_tables(tokens)
    table = jnp.concatenate([cos_t, sin_t], axis=0).astype(jnp.bfloat16)
    operands = jnp.concatenate([signal.astype(jnp.bfloat16), rows[:, 3]], axis=1)
    spec = jnp.dot(table, operands, preferred_element_type=jnp.float32)
    bins = tokens + 1
    sig_c, tap_c = (spec[:bins, :own], spec[:bins, own:])
    sig_s, tap_s = (spec[bins:, :own], spec[bins:, own:])
    weight = jnp.where((jnp.arange(bins) == 0) | (jnp.arange(bins) == tokens), 1.0, 2.0).astype(
        jnp.float32
    )[:, None] / (2 * tokens)
    real = (sig_c * tap_c - sig_s * tap_s) * weight
    turned = (sig_c * tap_s + sig_s * tap_c) * weight
    back = jnp.concatenate([real, turned], axis=0).astype(jnp.bfloat16)
    convolved = lax.dot_general(
        table, back, (((0,), (0,)), ((), ())), preferred_element_type=jnp.float32
    )
    output = (gating * (convolved + gain[None, :] * signal)).astype(jnp.bfloat16)
    return lax.all_to_all(output, "seq", split_axis=0, concat_axis=1, tiled=True)


def body(fresh, library, *rest):
    devices = lax.axis_size("seq")
    tokens = fresh.shape[0] * devices
    fits = tokens <= 4096 and fresh.shape[2] % devices == 0 and (library.shape[0] * BLK % 4 == 0)
    if fits:
        return local_body(fresh, library, *rest)
    return ring_body(fresh, library, *rest)


def solution(mesh):
    return jax.shard_map(
        body,
        mesh=mesh,
        in_specs=(
            P(("group", "seq"), None, "chan"),
            P("seq", None, "chan"),
            P(),
            P("group", None),
            P(None, None, "chan"),
            P("seq", "chan"),
            P("chan"),
        ),
        out_specs=P(("group", "seq"), "chan"),
        check_vma=False,
    )
```

profile of v0, /device:TPU:0, one launch (start us, length us, event | category | flops | bytes accessed | tf_op | source)
XLA Modules:
  0.0 86.8 jit_solution(6593084510004803457)
XLA Ops:
  0.0 0.0 copy-start
  0.0 0.0 copy-start.3
  0.0 0.8 reshape.169
  0.8 1.1 %convert_bitcast_fusion = bf16[128,1,1024]{2,0,1:T(8,128)(2,1)S(1)} fusion(f32[128,1024]{1,0:T(8,128)} %param.12), kind=kLoop, calls=%fused_computation.27 | loop fusion | flops 131072 | bytes 786432 | tf_op jit(solution)/shard_map/broadcast_in_dim | solution.py:153
  1.9 0.4 copy.37
  2.3 0.7 copy.38
  3.1 0.0 copy-done.3
  3.1 0.7 copy.36
  3.8 2.9 %pad_maximum_fusion.3 = bf16[130,4,1024]{0,1,2:T(4,128)(2,1)} fusion(bf16[2,4,1024]{0,1,2:T(4,128)(2,1)S(1)} %copy.38, bf16[128,1,1024]{0,1,2:T(2,128)(2,1)S(1)} %copy.37, bf16[128,3,1024]{0,1,2:T(4,128)(2,1)S(1)} %copy.36), kind=kLoop, calls=%fused_computation.6 | loop fusion | flops 3194880 | bytes 2129920 | tf_op jit(solution)/shard_map/concatenate | solution.py:154
  6.7 0.0 copy-start.4
  6.7 7.4 %all-to-all-start = ((bf16[130,4,1024]{0,1,2:T(4,128)(2,1)}), bf16[130,4,1024]{0,1,2:T(4,128)(2,1)S(1)}, u32[]{:S(2)}, u32[]{:S(2)}) async-start(bf16[130,4,1024]{0,1,2:T(4,128)(2,1)} %pad_maximum_fusion.3), calls=%async_computation | async-start | bytes 4194304 | tf_op jit(solution)/shard_map/all_to_all | solution.py:155
  14.1 0.0 copy-done.4
  14.1 0.1 copy.41
  14.2 0.1 reshape.171
  14.3 0.8 dynamic_slice.7
  15.0 0.0 copy-done
  15.0 0.7 gather_fusion
  15.7 0.7 dynamic-slice_bitcast_fusion.2
  16.5 0.6 fusion.25
  17.1 0.7 fusion.28
  17.7 3.7 %subtract_convert_fusion = (bf16[1025,32,32]{0,2,1:T(8,128)(2,1)}, bf16[1025,32,32]{0,2,1:T(8,128)(2,1)}) fusion(f32[1025,32]{0,1:T(8,128)S(1)} %get-tuple-element.14, f32[1025,32]{0,1:T(8,128)S(1)} %get-tuple-element.13, f32[1025,32]{0,1:T(8,128)S(1)} %get-tuple-element.15, f32[1025,32]{0,1:T(8,128)S(1)} %get-tuple-element.12), kind=kLoop, calls=%fused_computation.2 | loop fusion | flops 8396800 | bytes 4723200 | tf_op jit(solution)/shard_map/convert.5
  21.4 40.9 %all-to-all-done = bf16[130,4,1024]{0,1,2:T(4,128)(2,1)S(1)} async-done(((bf16[130,4,1024]{0,1,2:T(4,128)(2,1)}), bf16[130,4,1024]{0,1,2:T(4,128)(2,1)S(1)}, u32[]{:S(2)}, u32[]{:S(2)}) %all-to-all-start) | async-done | bytes 1064992 | tf_op jit(solution)/shard_map/all_to_all | solution.py:155
  62.3 3.9 %copy.43 = bf16[130,4,8,128]{3,2,1,0:T(8,128)(2,1)S(1)} copy(bf16[130,4,8,128]{0,1,3,2:T(4,128)(2,1)S(1)} %bitcast.44) | data formatting | bytes 2129920 | tf_op jit(solution)/shard_map/all_to_all | solution.py:155
  66.3 0.1 slice.70
  66.3 0.4 copy.40
  66.8 0.2 convolution_convert_fusion
  67.1 0.1 maximum_convert_fusion
  67.2 0.0 copy-start.1
  67.2 0.0 copy-start.2
  67.2 0.5 multiply_add_fusion
  67.8 0.1 fusion.12
  67.9 1.0 %copy-done.1 = bf16[1025,32,32]{0,2,1:T(8,128)(2,1)S(1)} copy-done((bf16[1025,32,32]{0,2,1:T(8,128)(2,1)S(1)}, bf16[1025,32,32]{0,2,1:T(8,128)(2,1)}, u32[]{:S(2)}) %copy-start.1) | copy-done | bytes 2099224
  68.9 0.7 copy-done.2
  69.6 2.2 %fusion.1 = f32[2050,256]{1,0:T(8,128)S(1)} fusion(bf16[1025,1024]{0,1:T(8,128)(2,1)S(1)} %bitcast.52, bf16[1025,1024]{0,1:T(8,128)(2,1)S(1)} %bitcast.50, bf16[1024,128]{1,0:T(8,128)(2,1)S(1)} %slice_bitcast_fusion.1, bf16[1024,128]{1,0:T(8,128)(2,1)S(1)} %fusion.12), kind=kOutput, calls=%fused_computation.5 | convolution fusion | flops 1084235776 | bytes 6821888 | tf_op jit(solution)/shard_map/dot_general | solution.py:179
  71.8 0.3 multiply_convert_fusion.1
  72.1 1.4 %fusion.4 = bf16[1024,128]{1,0:T(8,128)(2,1)S(1)} fusion(bf16[1025,1024]{0,1:T(8,128)(2,1)S(1)} %bitcast.53, bf16[1025,1024]{0,1:T(8,128)(2,1)S(1)} %bitcast.51, bf16[1025,128]{1,0:T(8,128)(2,1)S(1)} %get-tuple-element.6, bf16[1025,128]{1,0:T(8,128)(2,1)S(1)} %get-tuple-element.5, f32[1024,3,128]{2,0,1:T(8,128)S(1)} %multiply_add_fusion, ...), kind=kOutput, calls=%fused_computation.10 | convolution fusion | flops 547496960 | bytes 6558720 | tf_op jit(solution)/shard_map/dot_general | solution.py:189
  73.5 12.5 %all_to_all.34 = bf16[8,128,128]{2,1,0:T(8,128)(2,1)S(1)} all-to-all(bf16[8,128,128]{2,1,0:T(8,128)(2,1)S(1)} %bitcast.54), channel_id=1, replica_groups=mesh['group'=2,'seq'=8,'chan'=2] {'seq'}, dimensions={0} | all-to-all | bytes 524288 | tf_op jit(solution)/shard_map/all_to_all | solution.py:193
  86.0 0.7 copy_bitcast_fusion
  (10 shorter events, 0.1 us)
Async XLA Ops:
  0.0 15.0 %copy-start = (s32[8]{0:T(128)S(1)}, s32[8]{0:T(128)}, u32[]{:S(2)}) copy-start(s32[8]{0:T(128)} %param.9) | copy-start | bytes 100
  0.0 3.1 %copy-start.3 = (bf16[128,3,1024]{2,0,1:T(8,128)(2,1)S(1)}, bf16[128,3,1024]{2,0,1:T(8,128)(2,1)}, u32[]{:S(2)}) copy-start(bf16[128,3,1024]{2,0,1:T(8,128)(2,1)} %param.7) | copy-start | bytes 2359300
  6.7 7.4 %copy-start.4 = (s32[8,4]{0,1:T(4,128)S(1)}, s32[8,4]{0,1:T(4,128)}, u32[]{:S(2)}) copy-start(s32[8,4]{0,1:T(4,128)} %param.10) | copy-start | bytes 388
  6.7 55.7 %all-to-all-start = ((bf16[130,4,1024]{0,1,2:T(4,128)(2,1)}), bf16[130,4,1024]{0,1,2:T(4,128)(2,1)S(1)}, u32[]{:S(2)}, u32[]{:S(2)}) async-start(bf16[130,4,1024]{0,1,2:T(4,128)(2,1)} %pad_maximum_fusion.3), calls=%async_computation | async-start | bytes 4194304 | tf_op jit(solution)/shard_map/all_to_all | solution.py:155
  67.2 1.7 %copy-start.1 = (bf16[1025,32,32]{0,2,1:T(8,128)(2,1)S(1)}, bf16[1025,32,32]{0,2,1:T(8,128)(2,1)}, u32[]{:S(2)}) copy-start(bf16[1025,32,32]{0,2,1:T(8,128)(2,1)} %get-tuple-element.7) | copy-start | bytes 6297604
  67.2 2.4 %copy-start.2 = (bf16[1025,32,32]{0,2,1:T(8,128)(2,1)S(1)}, bf16[1025,32,32]{0,2,1:T(8,128)(2,1)}, u32[]{:S(2)}) copy-start(bf16[1025,32,32]{0,2,1:T(8,128)(2,1)} %get-tuple-element.8) | copy-start | bytes 6297604
where the time goes:
time: 87.2 us; the launch traced here: 86.8 us
  waiting for transfers between devices  40.9 us (47%)
  blocking collectives  12.5 us (14%)
  local copies, waits for them, and re-layouts  12 us (14%)
  other arithmetic  9.91 us (11%)
  starting transfers between devices  7.41 us (8%)
  matrix products  3.8 us (4%)
    all_to_all x1, waiting for transfers between devices, local_body(): lax.all_to_all(packed, 'seq', split_axis=2, concat_axis=0, tiled=True)  40.9 us
    all_to_all x1, blocking collectives, local_body(): lax.all_to_all(output, 'seq', split_axis=0, concat_axis=1, tiled=True)  12.5 us
    all_to_all x1, starting transfers between devices, local_body(): lax.all_to_all(packed, 'seq', split_axis=2, concat_axis=0, tiled=True)  7.41 us
    another operation x2, other arithmetic  3.99 us
    all_to_all x1, local copies, waits for them, and re-layouts, local_body(): lax.all_to_all(packed, 'seq', split_axis=2, concat_axis=0, tiled=True)  3.92 us
    concatenate x1, other arithmetic, local_body(): jnp.concatenate([packed, library.reshape(lib_rows, 4, channels)], axis=0)  2.86 us
    unnamed x12, local copies, waits for them, and re-layouts  2.58 us
    dot_general x1, matrix products, local_body(): spec = jnp.dot(table, operands, preferred_element_type=jnp.float32)  2.2 us
  transfers between devices with their start and end apart: 1, of which 1 were waited for; matrix products, arithmetic and copies ran while one was open for 8% of the time, Pallas kernels for 0%

commit v1 on v0

--- a/solution.py
+++ b/solution.py
@@ -152,7 +152,10 @@
     lib_rows = lib_here * BLK // 4
     packed = jnp.concatenate([fresh, long_filter.astype(jnp.bfloat16)[:, None, :]], axis=1)
     packed = jnp.concatenate([packed, library.reshape(lib_rows, 4, channels)], axis=0)
-    moved = lax.all_to_all(packed, "seq", split_axis=2, concat_axis=0, tiled=True)
+    moved = jnp.concatenate(
+        lax.all_to_all(jnp.stack(jnp.split(packed, lax.axis_size("seq"), axis=2)), "seq", 0, 0),
+        axis=0,
+    )
     moved = moved.reshape(devices, row_count + lib_rows, 4, own)
     rows = moved[:, :row_count].reshape(tokens, 4, own)
     lib_all = moved[:, row_count:].reshape(devices * lib_here, BLK * own)

time: 87.2 us -> 59.6 us (0.68)
  waiting for transfers between devices: 40.9 us -> 18.8 us
  local copies, waits for them, and re-layouts: 12 us -> 8.2 us
  other arithmetic: 9.91 us -> 8.27 us
    all_to_all x1, waiting for transfers between devices: 40.9 us -> 18.8 us  [local_body(): lax.all_to_all(jnp.stack(jnp.split(packed, lax.axis_size('seq'), axis=2))...]
    all_to_all x1 -> x0, local copies, waits for them, and re-layouts: 3.92 us -> none  [local_body(): lax.all_to_all(packed, 'seq', split_axis=2, concat_axis=0, tiled=True)]
    concatenate x1, other arithmetic: 2.86 us -> 1.25 us  [local_body(): jnp.concatenate([packed, library.reshape(lib_rows, 4, channels)], axis=0)]
    another operation x0 -> x2, local copies, waits for them, and re-layouts: none -> 1.48 us  [local_body(): jnp.stack(jnp.split(packed, lax.axis_size('seq'), axis=2))]
    unnamed x12 -> x17, local copies, waits for them, and re-layouts: 2.58 us -> 2.24 us
  transfers between devices with their start and end apart: 1 -> 1, of which waited for: 1 -> 1; matrix products, arithmetic and copies ran while one was open for 8% -> 12% of each run, Pallas kernels for 0% -> 0%
where the time goes in v1:
time: 59.6 us; the launch traced here: 59.2 us
  waiting for transfers between devices  18.8 us (32%)
  blocking collectives  12.5 us (21%)
  other arithmetic  8.27 us (14%)
  local copies, waits for them, and re-layouts  8.2 us (14%)
  starting transfers between devices  7.41 us (12%)
  matrix products  3.79 us (6%)
    all_to_all x1, waiting for transfers between devices, local_body(): lax.all_to_all(jnp.stack(jnp.split(packed, lax.axis_size('seq'), axis=2))...  18.8 us
    all_to_all x1, blocking collectives, local_body(): lax.all_to_all(output, 'seq', split_axis=0, concat_axis=1, tiled=True)  12.5 us
    all_to_all x1, starting transfers between devices, local_body(): lax.all_to_all(jnp.stack(jnp.split(packed, lax.axis_size('seq'), axis=2))...  7.41 us
    another operation x2, other arithmetic  3.96 us
    unnamed x17, local copies, waits for them, and re-layouts  2.24 us
    dot_general x1, matrix products, local_body(): spec = jnp.dot(table, operands, preferred_element_type=jnp.float32)  2.19 us
    another operation x2, local copies, waits for them, and re-layouts, local_body(): jnp.stack(jnp.split(packed, lax.axis_size('seq'), axis=2))  1.48 us
    dot_general x1, matrix products, local_body(): lax.dot_general(table, back, (((0,), (0,)), ((), ())), preferred_element_...  1.39 us
  transfers between devices with their start and end apart: 1, of which 1 were waited for; matrix products, arithmetic and copies ran while one was open for 12% of the time, Pallas kernels for 0%

profile of v1, /device:TPU:0, one launch (start us, length us, event | category | flops | bytes accessed | tf_op | source)
XLA Modules:
  0.0 59.2 jit_solution(14912400624332706978)
XLA Ops:
  0.0 0.0 copy-start
  0.0 0.7 %reshape.167 = bf16[2,4,1024]{2,1,0:T(4,128)(2,1)S(1)} reshape(bf16[1,8,1024]{2,1,0:T(8,128)(2,1)} %param.8) | data formatting | bytes 32768 | tf_op jit(solution)/shard_map/reshape | solution.py:154
  0.8 1.1 %convert_bitcast_fusion = bf16[128,1,1024]{2,0,1:T(8,128)(2,1)S(1)} fusion(f32[128,1024]{1,0:T(8,128)} %param.12), kind=kLoop, calls=%fused_computation.27 | loop fusion | flops 131072 | bytes 786432 | tf_op jit(solution)/shard_map/broadcast_in_dim | solution.py:153
  1.8 1.2 %pad_maximum_fusion.9 = bf16[130,4,1024]{2,0,1:T(8,128)(2,1)S(1)} fusion(bf16[2,4,1024]{2,0,1:T(2,128)(2,1)S(1)} %copy.32, bf16[128,1,1024]{2,0,1:T(8,128)(2,1)S(1)} %convert_bitcast_fusion, bf16[128,3,1024]{2,0,1:T(8,128)(2,1)} %param.7), kind=kLoop, calls=%fused_computation.11 | loop fusion | flops 3194880 | bytes 2129920 | tf_op jit(solution)/shard_map/concatenate | solution.py:154
  3.1 0.1 fusion.31
  3.2 0.1 fusion.30
  3.3 0.1 fusion.29
  3.3 0.1 fusion.28
  3.4 0.1 fusion.27
  3.4 0.1 fusion.26
  3.5 0.1 fusion.25
  3.6 1.4 %copy.33 = bf16[8,130,4,128]{3,2,1,0:T(4,128)(2,1)} copy(bf16[8,130,4,128]{3,1,2,0:T(8,128)(2,1)S(1)} %fusion.25) | data formatting | bytes 2129920 | tf_op jit(solution)/shard_map/stack | solution.py:156
  5.0 0.0 copy-start.3
  5.0 7.4 %all-to-all-start = ((bf16[8,130,4,128]{3,2,1,0:T(4,128)(2,1)}), bf16[8,130,4,128]{3,2,1,0:T(4,128)(2,1)S(1)}, u32[]{:S(2)}, u32[]{:S(2)}) async-start(bf16[8,130,4,128]{3,2,1,0:T(4,128)(2,1)} %copy.33), calls=%async_computation | async-start | bytes 2129920 | tf_op jit(solution)/shard_map/all_to_all | solution.py:156
  12.4 0.0 copy-done.3
  12.4 0.1 copy.35
  12.5 0.1 reshape.169
  12.6 0.8 %dynamic_slice.7 = f32[128]{0:T(128)S(1)} dynamic-slice(f32[1024]{0:T(1024)} %param.13, s32[]{:T(128)S(6)} %select_n.53), dynamic_slice_sizes={128} | dynamic-slice | bytes 1028 | tf_op jit(solution)/shard_map/dynamic_slice | solution.py:172
  13.3 0.0 copy-done
  13.4 0.7 %gather_fusion = s32[32]{0:T(128)S(1)} fusion(s32[8]{0:T(128)S(1)} %copy-done, s32[1024]{0:T(1024)S(1)} %pad_clamp_fusion), kind=kCustom, calls=%fused_computation | custom fusion | bytes 384 | tf_op jit(solution)/shard_map/gather | solution.py:162
  14.1 0.7 %dynamic-slice_bitcast_fusion.2 = (f32[3,128]{1,0:T(4,128)S(1)}, f32[3,128]{1,0:T(4,128)S(1)}, f32[3,128]{1,0:T(4,128)S(1)}) fusion(f32[3,3,1024]{2,1,0:T(4,128)} %param.11, s32[]{:T(128)S(6)} %select_n.53, s32[]{:T(128)S(6)} %add.79, s32[]{:T(128)S(6)} %add.80), kind=kLoop, calls=%fused_computation.78 | loop fusion | bytes 9228 | tf_op jit(solution)/shard_map/mul | solution.py:176
  14.8 0.6 fusion.33
  15.4 0.7 %fusion.36 = (f32[1025,32]{0,1:T(8,128)S(1)}, f32[1025,32]{0,1:T(8,128)S(1)}) fusion(s32[32]{0:T(128)S(1)} %iota_multiply_fusion), kind=kLoop, calls=%fused_computation.67 | loop fusion | flops 459200 | bytes 262528 | tf_op jit(solution)/shard_map/cos | solution.py:138
  16.0 3.7 %subtract_convert_fusion = (bf16[1025,32,32]{0,2,1:T(8,128)(2,1)}, bf16[1025,32,32]{0,2,1:T(8,128)(2,1)}) fusion(f32[1025,32]{0,1:T(8,128)S(1)} %get-tuple-element.14, f32[1025,32]{0,1:T(8,128)S(1)} %get-tuple-element.13, f32[1025,32]{0,1:T(8,128)S(1)} %get-tuple-element.15, f32[1025,32]{0,1:T(8,128)S(1)} %get-tuple-element.12), kind=kLoop, calls=%fused_computation.2 | loop fusion | flops 8396800 | bytes 4723200 | tf_op jit(solution)/shard_map/convert.5
  19.7 18.8 %all-to-all-done = bf16[8,130,4,128]{3,2,1,0:T(4,128)(2,1)S(1)} async-done(((bf16[8,130,4,128]{3,2,1,0:T(4,128)(2,1)}), bf16[8,130,4,128]{3,2,1,0:T(4,128)(2,1)S(1)}, u32[]{:S(2)}, u32[]{:S(2)}) %all-to-all-start) | async-done | bytes 1064992 | tf_op jit(solution)/shard_map/all_to_all | solution.py:156
  38.5 0.4 slice.70
  38.9 0.2 copy.34
  39.3 0.2 convolution_convert_fusion
  39.5 0.1 maximum_convert_fusion
  39.6 0.0 copy-start.1
  39.7 0.0 copy-start.2
  39.7 0.5 multiply_add_fusion
  40.2 0.1 fusion.12
  40.3 1.0 %copy-done.1 = bf16[1025,32,32]{0,2,1:T(8,128)(2,1)S(1)} copy-done((bf16[1025,32,32]{0,2,1:T(8,128)(2,1)S(1)}, bf16[1025,32,32]{0,2,1:T(8,128)(2,1)}, u32[]{:S(2)}) %copy-start.1) | copy-done | bytes 2099224
  41.3 0.7 %copy-done.2 = bf16[1025,32,32]{0,2,1:T(8,128)(2,1)S(1)} copy-done((bf16[1025,32,32]{0,2,1:T(8,128)(2,1)S(1)}, bf16[1025,32,32]{0,2,1:T(8,128)(2,1)}, u32[]{:S(2)}) %copy-start.2) | copy-done | bytes 2099224
  42.0 2.2 %fusion.1 = f32[2050,256]{1,0:T(8,128)S(1)} fusion(bf16[1025,1024]{0,1:T(8,128)(2,1)S(1)} %bitcast.79, bf16[1025,1024]{0,1:T(8,128)(2,1)S(1)} %bitcast.77, bf16[1024,128]{1,0:T(8,128)(2,1)S(1)} %slice_bitcast_fusion.1, bf16[1024,128]{1,0:T(8,128)(2,1)S(1)} %fusion.12), kind=kOutput, calls=%fused_computation.5 | convolution fusion | flops 1084235776 | bytes 6821888 | tf_op jit(solution)/shard_map/dot_general | solution.py:182
  44.2 0.3 multiply_convert_fusion.1
  44.5 1.4 %fusion.4 = bf16[1024,128]{1,0:T(8,128)(2,1)S(1)} fusion(bf16[1025,1024]{0,1:T(8,128)(2,1)S(1)} %bitcast.80, bf16[1025,1024]{0,1:T(8,128)(2,1)S(1)} %bitcast.78, bf16[1025,128]{1,0:T(8,128)(2,1)S(1)} %get-tuple-element.6, bf16[1025,128]{1,0:T(8,128)(2,1)S(1)} %get-tuple-element.5, f32[1024,3,128]{2,0,1:T(8,128)S(1)} %multiply_add_fusion, ...), kind=kOutput, calls=%fused_computation.9 | convolution fusion | flops 547496960 | bytes 6558720 | tf_op jit(solution)/shard_map/dot_general | solution.py:192
  45.9 12.5 %all_to_all.24 = bf16[8,128,128]{2,1,0:T(8,128)(2,1)S(1)} all-to-all(bf16[8,128,128]{2,1,0:T(8,128)(2,1)S(1)} %bitcast.81), channel_id=1, replica_groups=mesh['group'=2,'seq'=8,'chan'=2] {'seq'}, dimensions={0} | all-to-all | bytes 524288 | tf_op jit(solution)/shard_map/all_to_all | solution.py:196
  58.4 0.7 %copy_bitcast_fusion = bf16[128,1024]{1,0:T(8,128)(2,1)} fusion(bf16[8,128,128]{2,1,0:T(8,128)(2,1)S(1)} %all_to_all.24), kind=kLoop, calls=%fused_computation.24 | loop fusion | bytes 524288 | tf_op jit(solution)/shard_map/all_to_all | solution.py:196
  (13 shorter events, 0.2 us)
Async XLA Ops:
  0.0 13.3 %copy-start = (s32[8]{0:T(128)S(1)}, s32[8]{0:T(128)}, u32[]{:S(2)}) copy-start(s32[8]{0:T(128)} %param.9) | copy-start | bytes 100
  5.0 7.4 %copy-start.3 = (s32[8,4]{0,1:T(4,128)S(1)}, s32[8,4]{0,1:T(4,128)}, u32[]{:S(2)}) copy-start(s32[8,4]{0,1:T(4,128)} %param.10) | copy-start | bytes 388
  5.0 33.5 %all-to-all-start = ((bf16[8,130,4,128]{3,2,1,0:T(4,128)(2,1)}), bf16[8,130,4,128]{3,2,1,0:T(4,128)(2,1)S(1)}, u32[]{:S(2)}, u32[]{:S(2)}) async-start(bf16[8,130,4,128]{3,2,1,0:T(4,128)(2,1)} %copy.33), calls=%async_computation | async-start | bytes 2129920 | tf_op jit(solution)/shard_map/all_to_all | solution.py:156
  39.6 1.7 %copy-start.1 = (bf16[1025,32,32]{0,2,1:T(8,128)(2,1)S(1)}, bf16[1025,32,32]{0,2,1:T(8,128)(2,1)}, u32[]{:S(2)}) copy-start(bf16[1025,32,32]{0,2,1:T(8,128)(2,1)} %get-tuple-element.7) | copy-start | bytes 6297604
  39.7 2.4 %copy-start.2 = (bf16[1025,32,32]{0,2,1:T(8,128)(2,1)S(1)}, bf16[1025,32,32]{0,2,1:T(8,128)(2,1)}, u32[]{:S(2)}) copy-start(bf16[1025,32,32]{0,2,1:T(8,128)(2,1)} %get-tuple-element.8) | copy-start | bytes 6297604
